TPU v7x, 128 devices: a whole 4x4x4 slice. The times are simulated.
128 devices in a mesh: px: 8 (over x_lo, z), py: 16 (over x_hi, y, core).
Axes of the slice: x: 4 (x_hi: 2, x_lo: 2; x = x_hi * 2 + x_lo), y: 4, z: 4, core: 2. Of those that a mesh axis runs over, the one named last changes fastest.
Arguments:
- widths: float32 [2048, 4096], P('px', 'py'), may hold values from -1 to 1
- couplings: int32 [256, 512, 9], P('px', 'py'), may hold values 0 or 1
- surrogate: bfloat16 [9, 256, 1024], replicated, may hold values from -0.375 to 0.375
- target_far: bfloat16 [2048, 8, 2, 512], P(('px', 'py')), may hold values from -6 to 6
Outputs:
- far_field: float32 [2048, 8, 2, 512], P(('px', 'py'))
- width_grad: float32 [2048, 4096], P('px', 'py')
All inputs are finite; a program needn't handle non-finite values. No bound on the sum of `couplings` on one device may be relied on, other than what follows from the above.
Results may differ from a plain program's by a relative error of at most 0.0033.
The roundings to bfloat16 on the way count: a program that leaves them out, or rounds other values in their place, can miss the bound.
Values may be sent and summed in bfloat16 or wider, within the bound.
No kernel may reach another device: no remote copies, remote signals or barrier semaphores. Data moves between devices by JAX's collectives and lax.ppermute only.
A program may use at most 128 MiB of HBM per device.

v0:
```python
import math

import jax
import jax.numpy as jnp
from jax import lax
from jax.sharding import PartitionSpec as P

BS = 8
NF = 4
NW = 8
NK = 512
FEAT = 256
OUTS = 1024


tv_weight = 0.5
tv_floor = 0.01


def with_halo(block, sides, width):
    for axis, dim in sides:
        count = lax.axis_size(axis)
        forward = [(i, i + 1) for i in range(count - 1)]
        backward = [(target, source) for source, target in forward]
        low = lax.ppermute(
            lax.slice_in_dim(block, block.shape[dim] - width, None, axis=dim), axis, forward
        )
        high = lax.ppermute(lax.slice_in_dim(block, 0, width, axis=dim), axis, backward)
        block = jnp.concatenate([low, block, high], axis=dim)
    return block


def chebyshev(normed, levels):
    values, slopes = ([], [])
    before = jnp.ones_like(normed)
    current = normed
    slope_before = jnp.zeros_like(normed)
    slope_now = jnp.ones_like(normed)
    for level in range(levels):
        values.append(current)
        slopes.append(slope_now)
        follow = 2.0 * normed * current - before
        slope_follow = 2.0 * current + 2.0 * normed * slope_now - slope_before
        before, current, slope_before, slope_now = (current, follow, slope_now, slope_follow)
    return (jnp.stack(values, 1), jnp.stack(slopes, 1))


def cell_blocks(planes, block_side):
    height, layers, columns = planes.shape
    shaped = planes.reshape(
        height // block_side, block_side, layers, columns // block_side, block_side
    )
    return shaped.transpose(0, 3, 1, 2, 4).reshape(
        height // block_side, columns // block_side, block_side * layers * block_side
    )


def block_cells(blocks, block_side, layers):
    block_rows, block_cols, unused = blocks.shape
    shaped = blocks.reshape(block_rows, block_cols, block_side, layers, block_side)
    return shaped.transpose(0, 2, 3, 1, 4).reshape(
        block_rows * block_side, layers, block_cols * block_side
    )


def field_rows(blocks, block_side, wave_count):
    block_rows, block_cols, unused = blocks.shape
    shaped = blocks.reshape(block_rows, block_cols, block_side, wave_count, 2 * block_side)
    return shaped.transpose(0, 2, 3, 1, 4).reshape(
        block_rows * block_side * wave_count, block_cols * 2 * block_side
    )


def rows_field(row_flat, block_side, wave_count):
    row_count, unused = row_flat.shape
    height = row_count // wave_count
    block_cols = unused // (2 * block_side)
    shaped = row_flat.reshape(
        height // block_side, block_side, wave_count, block_cols, 2 * block_side
    )
    return shaped.transpose(0, 3, 1, 2, 4).reshape(
        height // block_side, block_cols, block_side * wave_count * 2 * block_side
    )


def phase_table(first_col, col_count, total_cols):
    places = first_col + jnp.arange(col_count, dtype=jnp.int32)
    orders = jnp.arange(NK, dtype=jnp.int32) - NK // 2
    phase_turns = places[:, None] * orders[None, :] % total_cols
    angles = phase_turns.astype(jnp.float32) * (2.0 * math.pi / total_cols)
    cosine = jnp.cos(angles)
    sine_part = jnp.sin(angles)
    phase_rows = jnp.stack(
        [jnp.stack([cosine, -sine_part], 1), jnp.stack([sine_part, cosine], 1)], 1
    )
    phase_rows = phase_rows.astype(jnp.bfloat16).reshape(col_count // BS, BS, 2, 2 * NK)
    return phase_rows.transpose(0, 2, 1, 3).reshape(2 * col_count, 2 * NK)


def variation(framed, row_first, col_first, total_rows, total_cols):
    height = framed.shape[0] - 2
    columns = framed.shape[1] - 2
    step_down = framed[1:, :-1] - framed[:-1, :-1]
    step_right = framed[:-1, 1:] - framed[:-1, :-1]
    row_at = row_first - 1 + jnp.arange(height + 1, dtype=jnp.int32)
    col_at = col_first - 1 + jnp.arange(columns + 1, dtype=jnp.int32)
    step_down = jnp.where(((row_at >= 0) & (row_at < total_rows - 1))[:, None], step_down, 0.0)
    step_right = jnp.where(((col_at >= 0) & (col_at < total_cols - 1))[None, :], step_right, 0.0)
    magnitude = jnp.sqrt(step_down * step_down + step_right * step_right + tv_floor)
    flow_down = step_down / magnitude
    flow_right = step_right / magnitude
    return -(flow_down + flow_right)[1:, 1:] + flow_down[:-1, 1:] + flow_right[1:, :-1]


def per_device(widths, couplings, surrogate, target_far):
    height, columns = widths.shape
    block_rows = height // BS
    block_cols = columns // BS
    total_cols = columns * lax.axis_size("py")
    total_rows = height * lax.axis_size("px")
    mask_cells = jnp.pad(couplings.astype(jnp.float32), ((0, 0), (0, 0), (0, BS * BS - 9)))
    mask_cells = (
        mask_cells.reshape(block_rows, block_cols, BS, BS)
        .transpose(0, 2, 1, 3)
        .reshape(height, columns)
    )
    rimmed = with_halo(jnp.stack([widths, mask_cells]), (("px", 1), ("py", 2)), BS)
    wide_widths = rimmed[0]
    wide_mask = rimmed[1].reshape(block_rows + 2, BS, block_cols + 2, BS).transpose(0, 2, 1, 3)
    wide_mask = wide_mask.reshape(block_rows + 2, block_cols + 2, BS * BS)
    values, slopes = chebyshev(wide_widths, NF)
    own_slopes = slopes[BS : BS + height, :, BS : BS + columns]
    features = cell_blocks(values, BS).astype(jnp.bfloat16)
    gathered = jnp.zeros((block_rows, block_cols, OUTS), jnp.float32)
    for row_step in range(3):
        for col_step in range(3):
            offset = row_step * 3 + col_step
            source = features[
                2 - row_step : 2 - row_step + block_rows, 2 - col_step : 2 - col_step + block_cols
            ]
            product = jnp.dot(
                source.reshape(block_rows * block_cols, FEAT),
                surrogate[offset],
                preferred_element_type=jnp.float32,
            )
            flags = wide_mask[
                2 - row_step : 2 - row_step + block_rows,
                2 - col_step : 2 - col_step + block_cols,
                offset,
            ]
            gathered = gathered + flags[:, :, None] * product.reshape(block_rows, block_cols, OUTS)
    near_field = gathered.astype(jnp.bfloat16)
    row_flat = field_rows(near_field, BS, NW)
    norm_scale = 1.0 / math.sqrt(total_cols)
    local_table = phase_table(lax.axis_index("py") * columns, columns, total_cols)
    part_rows = row_flat
    flat_rows = jnp.dot(part_rows, local_table, preferred_element_type=jnp.float32)
    far_field = lax.psum_scatter(
        (flat_rows * norm_scale).reshape(
            height // lax.axis_size("py") * lax.axis_size("py"), NW, 2, NK
        ),
        "py",
        scatter_dimension=0,
        tiled=True,
    )
    far_miss = (far_field - target_far.astype(jnp.float32)).astype(jnp.bfloat16)
    part_rows = lax.all_gather(far_miss, "py", axis=0, tiled=True)
    flat_rows = jnp.dot(
        part_rows.reshape(part_rows.shape[0] * NW, 2 * NK),
        local_table.T,
        preferred_element_type=jnp.float32,
    )
    adj_flat = (flat_rows * norm_scale).astype(jnp.bfloat16)
    adj_blocks = rows_field(adj_flat, BS, NW)
    wide_adj = with_halo(adj_blocks, (("px", 0), ("py", 1)), 1)
    feat_grad = jnp.zeros((block_rows, block_cols, FEAT), jnp.float32)
    for row_step in range(3):
        for col_step in range(3):
            offset = row_step * 3 + col_step
            targets_at = wide_adj[
                row_step : row_step + block_rows, col_step : col_step + block_cols
            ]
            product = jnp.dot(
                targets_at.reshape(block_rows * block_cols, OUTS),
                surrogate[offset].T,
                preferred_element_type=jnp.float32,
            )
            flags = couplings[:, :, offset].astype(jnp.float32)
            feat_grad = feat_grad + flags[:, :, None] * product.reshape(
                block_rows, block_cols, FEAT
            )
    planes = block_cells(feat_grad, BS, NF)
    near_grad = jnp.sum(planes * own_slopes, axis=1)
    framed = with_halo(widths.astype(jnp.bfloat16), (("px", 0), ("py", 1)), 1).astype(widths.dtype)
    grad_tv = variation(
        framed,
        lax.axis_index("px") * height,
        lax.axis_index("py") * columns,
        total_rows,
        total_cols,
    )
    return (far_field, near_grad + tv_weight * grad_tv)


def solution(mesh):
    return jax.shard_map(
        per_device,
        mesh=mesh,
        in_specs=(P("px", "py"), P("px", "py", None), P(), P(("px", "py"), None, None, None)),
        out_specs=(P(("px", "py"), None, None, None), P("px", "py")),
        check_vma=False,
    )
```

profile of v0, /device:TPU:27, one launch (start us, length us, event | category | flops | bytes accessed | tf_op | source)
XLA Modules:
  0.0 448.7 jit_solution(1752436421931998768)
XLA Ops:
  8.3 2.7 copy.128
  11.0 4.0 stack_reshape.3
  15.1 3.5 collective-permute-start
  18.6 4.0 collective-permute-start.1
  22.7 2.5 negate_convert_fusion
  27.3 4.5 %collective-permute-start.2 = (f32[2,272,8]{2,1,0:T(8,128)S(1)}, f32[2,272,8]{2,1,0:T(8,128)S(1)}, u32[]{:S(2)}, u32[]{:S(2)}) collective-permute-start(f32[2,272,8]{2,1,0:T(8,128)S(1)} %get-tuple-element.31), channel_id=1, source_target_pairs={{0,1},{1,2},{2,3},{3,4},{4,5},{5,6},{6,7},{7,8},{8,9},{9,10},{10,1... | collective-permute-start | bytes 52232 | tf_op jit(solution)/shard_map/ppermute | solution.py:25
  31.8 1.9 collective-permute-start.3
  35.3 8.0 %collective-permute-done.3 = f32[2,272,8]{2,1,0:T(8,128)S(1)} collective-permute-done((f32[2,272,8]{2,1,0:T(8,128)S(1)}, f32[2,272,8]{2,1,0:T(8,128)S(1)}, u32[]{:S(2)}, u32[]{:S(2)}) %collective-permute-start.3) | collective-permute-done | bytes 17440 | tf_op jit(solution)/shard_map/ppermute | solution.py:28
  44.6 3.2 stack.43
  47.9 5.3 %copy.130 = f32[34,8,1,34,8]{3,4,2,1,0:T(8,128)} copy(f32[34,8,1,34,8]{4,3,1,0,2:T(8,128)} %stack.43) | data formatting | bytes 591872 | tf_op jit(solution)/shard_map/stack | solution.py:45
  53.1 3.1 convert.26
  56.2 4.0 copy.133
  63.8 4.7 %fusion.21 = f32[32,32,1024]{2,1,0:T(8,128)} fusion(bf16[34,34,256]{1,2,0:T(8,128)(2,1)S(1)} %bitcast.126, bf16[9,256,1024]{2,1,0:T(8,128)(2,1)} %param.6), kind=kOutput, calls=%fused_computation.27 | convolution fusion | flops 536870912 | bytes 6815744 | tf_op jit(solution)/shard_map/dot_general | solution.py:141
  68.4 3.7 fusion.23
  72.1 3.0 fusion.25
  75.1 3.6 fusion.27
  78.8 3.6 fusion.29
  82.4 3.1 fusion.31
  85.5 3.6 fusion.33
  89.0 3.6 fusion.35
  92.6 3.2 reshape_squeeze.3
  95.8 5.4 %copy.129 = f32[34,34,8,8]{1,3,2,0:T(8,128)} copy(f32[34,34,8,8]{3,1,2,0:T(8,128)} %bitcast.140) | data formatting | bytes 591872 | tf_op jit(solution)/shard_map/transpose | solution.py:129
  103.1 13.8 %add_convert_fusion = bf16[32,32,1024]{2,1,0:T(8,128)(2,1)} fusion(f32[32,32,1024]{2,1,0:T(8,128)} %fusion.21, f32[32,32,1024]{2,1,0:T(8,128)} %fusion.23, f32[32,32,1024]{2,1,0:T(8,128)} %fusion.25, f32[32,32,1024]{2,1,0:T(8,128)} %fusion.27, f32[32,32,1024]{2,1,0:T(8,128)} %fusion.29, f32[32,32,1024]{2,1,0:T(8,128)} %fusion.31, ...), kind=kOutput, calls=%fused_computation.2 | convolution fusion | flops 555745280 | bytes 38420480 | tf_op jit(solution)/shard_map/dot_general | solution.py:141
  116.9 7.8 %copy.143 = bf16[32,32,1024]{1,2,0:T(8,128)(2,1)} copy(bf16[32,32,1024]{2,1,0:T(8,128)(2,1)} %add_convert_fusion) | data formatting | bytes 4194304 | tf_op jit(solution)/shard_map/convert_element_type | solution.py:152
  124.7 15.8 %copy.144 = bf16[32,8,8,32,16]{4,3,2,1,0:T(8,128)(2,1)} copy(bf16[32,8,8,32,16]{3,4,2,1,0:T(8,128)(2,1)} %bitcast.139) | data formatting | bytes 4194304 | tf_op jit(solution)/shard_map/transpose | solution.py:69
  140.5 27.9 %reshape.450 = bf16[2048,512]{1,0:T(8,128)(2,1)S(1)} reshape(bf16[32,8,8,32,16]{4,3,2,1,0:T(8,128)(2,1)} %copy.144) | data formatting | bytes 4194304 | tf_op jit(solution)/shard_map/reshape | solution.py:69
  168.4 6.9 %convolution_multiply_fusion = f32[2048,1024]{1,0:T(8,128)} fusion(bf16[2048,512]{1,0:T(8,128)(2,1)S(1)} %reshape.450, bf16[512,1024]{1,0:T(8,128)(2,1)} %bitcast.155), kind=kOutput, calls=%fused_computation | convolution fusion | flops 2149580800 | bytes 11534336 | tf_op jit(solution)/shard_map/dot_general | solution.py:157
  175.4 96.9 %reduce-scatter.2.cloned.1.call-done = f32[16,8,2,512]{3,1,2,0:T(8,128)} async-done(((f32[256,8,2,512]{3,1,2,0:T(8,128)}), f32[16,8,2,512]{3,1,2,0:T(8,128)}) %reduce-scatter.2.cloned.1.call-update) | async-done | bytes 524304 | tf_op jit(solution)/shard_map/reduce_scatter | solution.py:158
  274.2 3.2 collective-permute-start.8
  277.5 4.2 collective-permute-start.9
  282.5 6.7 %collective-permute-start.10 = (bf16[258,1]{1,0:T(8,128)(2,1)S(1)}, bf16[258,1]{1,0:T(8,128)(2,1)S(1)}, u32[]{:S(2)}, u32[]{:S(2)}) collective-permute-start(bf16[258,1]{1,0:T(8,128)(2,1)S(1)} %get-tuple-element.48), channel_id=1, source_target_pairs={{0,1},{1,2},{2,3},{3,4},{4,5},{5,6},{6,7},{7,8},{8,9},{9,10},{10,1... | collective-permute-start | bytes 1556 | tf_op jit(solution)/shard_map/ppermute | solution.py:25
  291.6 6.9 %collective-permute-done.11 = bf16[258,1]{1,0:T(8,128)(2,1)S(1)} collective-permute-done((bf16[258,1]{1,0:T(8,128)(2,1)S(1)}, bf16[258,1]{1,0:T(8,128)(2,1)S(1)}, u32[]{:S(2)}, u32[]{:S(2)}) %collective-permute-start.11) | collective-permute-done | bytes 548 | tf_op jit(solution)/shard_map/ppermute | solution.py:28
  302.2 28.5 %all-gather.2.cloned.1.call-done = bf16[256,8,2,512]{3,1,2,0:T(8,128)(2,1)} async-done(((bf16[16,8,2,512]{3,1,2,0:T(8,128)(2,1)}), bf16[256,8,2,512]{3,1,2,0:T(8,128)(2,1)}) %all-gather.2.cloned.1.call-update) | async-done | bytes 4194320 | tf_op jit(solution)/shard_map/all_gather | solution.py:167
  330.7 4.9 %multiply_convert_fusion = bf16[2048,512]{1,0:T(8,128)(2,1)S(1)} fusion(bf16[2048,1024]{1,0:T(8,128)(2,1)} %bitcast.166, bf16[512,1024]{1,0:T(8,128)(2,1)} %bitcast.156), kind=kOutput, calls=%fused_computation.1 | convolution fusion | flops 2149580800 | bytes 7340032 | tf_op jit(solution)/shard_map/dot_general | solution.py:168
  335.6 15.5 %reshape.454 = bf16[32,8,8,32,16]{4,3,2,1,0:T(8,128)(2,1)} reshape(bf16[2048,512]{1,0:T(8,128)(2,1)S(1)} %multiply_convert_fusion) | data formatting | bytes 4194304 | tf_op jit(solution)/shard_map/reshape | solution.py:78
  352.3 16.0 %copy.151 = bf16[32,32,8,8,16]{1,4,3,2,0:T(8,128)(2,1)} copy(bf16[32,32,8,8,16]{4,1,3,2,0:T(8,128)(2,1)} %bitcast.138) | data formatting | bytes 4194304 | tf_op jit(solution)/shard_map/transpose | solution.py:81
  369.3 3.4 collective-permute-start.4
  373.7 4.2 collective-permute-start.5
  377.9 5.9 %convolution_multiply_fusion.1 = f32[32,32,256]{2,1,0:T(8,128)S(1)} fusion(bf16[32,32,1024]{1,2,0:T(8,128)(2,1)} %bitcast.135, f32[32,32]{1,0:T(8,128)S(1)} %copy-done.10, bf16[9,256,1024]{2,1,0:T(8,128)(2,1)} %param.6), kind=kOutput, calls=%fused_computation.47 | convolution fusion | flops 537133056 | bytes 9965568 | tf_op jit(solution)/shard_map/dot_general | solution.py:183
  383.8 6.7 %copy.154 = bf16[32,32,1024]{2,1,0:T(8,128)(2,1)S(1)} copy(bf16[32,32,1024]{1,2,0:T(8,128)(2,1)} %bitcast.136) | data formatting | bytes 4194304 | tf_op jit(solution)/shard_map/reshape | solution.py:81
  391.5 5.1 %collective-permute-start.6 = (bf16[34,1,1024]{2,1,0:T(2,128)(2,1)S(1)}, bf16[34,1,1024]{2,1,0:T(2,128)(2,1)S(1)}, u32[]{:S(2)}, u32[]{:S(2)}) collective-permute-start(bf16[34,1,1024]{2,1,0:T(2,128)(2,1)S(1)} %get-tuple-element.12), channel_id=1, source_target_pairs={{0,1},{1,2},{2,3},{3,4},{4,5},{5,6},{6,7},{7,8},{8,9},{9,10},{10,1... | collective-permute-start | bytes 208904 | tf_op jit(solution)/shard_map/ppermute | solution.py:25
  396.6 1.9 collective-permute-start.7
  400.4 2.0 fusion.41
  402.4 4.2 collective-permute-done.7
  406.6 2.5 maximum_maximum_fusion
  414.2 2.7 copy.158
  416.9 10.6 %copy.159 = f32[32,8,4,32,8]{4,3,1,0,2:T(8,128)} copy(f32[32,8,4,32,8]{3,4,2,1,0:T(8,128)} %bitcast.141) | data formatting | bytes 2097152 | tf_op jit(solution)/shard_map/transpose | solution.py:61
  427.5 12.8 %reshape.457 = f32[256,4,256]{2,0,1:T(8,128)S(1)} reshape(f32[32,8,4,32,8]{4,3,1,0,2:T(8,128)} %copy.159) | data formatting | bytes 2097152 | tf_op jit(solution)/shard_map/reshape | solution.py:61
  (106 shorter events, 32.6 us)
Async XLA Ops:
  7.2 265.1 %reduce-scatter.2.cloned.1.call-start = ((), (), s32[]{:S(2)}) async-start(), calls=%async_computation.1 | async-start | bytes 8912896 | tf_op jit(solution)/shard_map/reduce_scatter | solution.py:158
  8.3 6.8 %copy-start.2 = (f32[256,256]{1,0:T(8,128)S(1)}, f32[256,256]{1,0:T(8,128)}, u32[]{:S(2)}) copy-start(f32[256,256]{1,0:T(8,128)} %param.4) | copy-start | bytes 786436
  15.1 12.0 %collective-permute-start = (f32[2,8,256]{2,1,0:T(8,128)S(1)}, f32[2,8,256]{2,1,0:T(8,128)S(1)}, u32[]{:S(2)}, u32[]{:S(2)}) collective-permute-start(f32[2,8,256]{2,1,0:T(8,128)S(1)} %get-tuple-element.33), channel_id=1, source_target_pairs={{0,16},{16,32},{32,48},{48,64},{64,80},{80,96},{96,112},{1,17},{17... | collective-permute-start | bytes 49160 | tf_op jit(solution)/shard_map/ppermute | solution.py:25
  18.6 8.5 %collective-permute-start.1 = (f32[2,8,256]{2,1,0:T(8,128)S(1)}, f32[2,8,256]{2,1,0:T(8,128)S(1)}, u32[]{:S(2)}, u32[]{:S(2)}) collective-permute-start(f32[2,8,256]{2,1,0:T(8,128)S(1)} %get-tuple-element.34), channel_id=1, source_target_pairs={{16,0},{32,16},{48,32},{64,48},{80,64},{96,80},{112,96},{17,1},{33... | collective-permute-start | bytes 49160 | tf_op jit(solution)/shard_map/ppermute | solution.py:28
  27.3 8.0 %collective-permute-start.2 = (f32[2,272,8]{2,1,0:T(8,128)S(1)}, f32[2,272,8]{2,1,0:T(8,128)S(1)}, u32[]{:S(2)}, u32[]{:S(2)}) collective-permute-start(f32[2,272,8]{2,1,0:T(8,128)S(1)} %get-tuple-element.31), channel_id=1, source_target_pairs={{0,1},{1,2},{2,3},{3,4},{4,5},{5,6},{6,7},{7,8},{8,9},{9,10},{10,1... | collective-permute-start | bytes 52232 | tf_op jit(solution)/shard_map/ppermute | solution.py:25
  31.8 11.5 %collective-permute-start.3 = (f32[2,272,8]{2,1,0:T(8,128)S(1)}, f32[2,272,8]{2,1,0:T(8,128)S(1)}, u32[]{:S(2)}, u32[]{:S(2)}) collective-permute-start(f32[2,272,8]{2,1,0:T(8,128)S(1)} %get-tuple-element.32), channel_id=1, source_target_pairs={{1,0},{2,1},{3,2},{4,3},{5,4},{6,5},{7,6},{8,7},{9,8},{10,9},{11,1... | collective-permute-start | bytes 52232 | tf_op jit(solution)/shard_map/ppermute | solution.py:28
  43.7 0.9 copy-start
  60.2 8.2 %slice-start = ((s8[4718592]{0:T(1024)(128)(4,1)}), s8[4194304]{0:T(1024)(128)(4,1)S(1)}, s32[]{:S(2)}) async-start(s8[4718592]{0:T(1024)(128)(4,1)} %bitcast.144), calls=%async_computation.3 | async-start | bytes 8388608
  62.0 6.4 %slice-start.1 = ((s8[4718592]{0:T(1024)(128)(4,1)}), s8[524288]{0:T(1024)(128)(4,1)S(1)}, s32[]{:S(2)}) async-start(s8[4718592]{0:T(1024)(128)(4,1)} %bitcast.144), calls=%async_computation.4 | async-start | bytes 1048576
  175.3 97.0 %copy-start.9 = (bf16[16,8,2,512]{3,2,1,0:T(2,128)(2,1)S(1)}, bf16[16,8,2,512]{3,2,1,0:T(2,128)(2,1)}, u32[]{:S(2)}) copy-start(bf16[16,8,2,512]{3,2,1,0:T(2,128)(2,1)} %param.7) | copy-start | bytes 786436
  175.3 106.4 %copy-start.8 = (s32[32,32,9]{1,0,2:T(8,128)S(1)}, s32[32,32,9]{1,0,2:T(8,128)}, u32[]{:S(2)}) copy-start(s32[32,32,9]{1,0,2:T(8,128)} %param.5) | copy-start | bytes 110596
  175.3 124.4 %copy-start.1 = (f32[2,272,272]{2,1,0:T(8,128)S(1)}, f32[2,272,272]{2,1,0:T(8,128)}, u32[]{:S(2)}) copy-start(f32[2,272,272]{2,1,0:T(8,128)} %copy-done) | copy-start | bytes 1775620
  175.3 155.4 %all-gather.2.cloned.1.call-start = ((), (), s32[]{:S(2)}) async-start(), calls=%async_computation.2 | async-start | bytes 4456448 | tf_op jit(solution)/shard_map/all_gather | solution.py:167
  272.3 28.8 %copy-start.4 = (f32[16,8,2,512]{3,1,2,0:T(8,128)S(1)}, f32[16,8,2,512]{3,1,2,0:T(8,128)}, u32[]{:S(2)}) copy-start(f32[16,8,2,512]{3,1,2,0:T(8,128)} %reduce-scatter.2.cloned.1.call-done) | copy-start | bytes 1572868
  274.2 8.1 %collective-permute-start.8 = (bf16[1,256]{1,0:T(2,128)(2,1)S(1)}, bf16[1,256]{1,0:T(2,128)(2,1)S(1)}, u32[]{:S(2)}, u32[]{:S(2)}) collective-permute-start(bf16[1,256]{1,0:T(2,128)(2,1)S(1)} %get-tuple-element.50), channel_id=1, source_target_pairs={{0,16},{16,32},{32,48},{48,64},{64,80},{80,96},{96,112},{1,17},{17... | collective-permute-start | bytes 1544 | tf_op jit(solution)/shard_map/ppermute | solution.py:25
  277.5 4.9 %collective-permute-start.9 = (bf16[1,256]{1,0:T(2,128)(2,1)S(1)}, bf16[1,256]{1,0:T(2,128)(2,1)S(1)}, u32[]{:S(2)}, u32[]{:S(2)}) collective-permute-start(bf16[1,256]{1,0:T(2,128)(2,1)S(1)} %get-tuple-element.51), channel_id=1, source_target_pairs={{16,0},{32,16},{48,32},{64,48},{80,64},{96,80},{112,96},{17,1},{33... | collective-permute-start | bytes 1544 | tf_op jit(solution)/shard_map/ppermute | solution.py:28
  282.5 9.1 %collective-permute-start.10 = (bf16[258,1]{1,0:T(8,128)(2,1)S(1)}, bf16[258,1]{1,0:T(8,128)(2,1)S(1)}, u32[]{:S(2)}, u32[]{:S(2)}) collective-permute-start(bf16[258,1]{1,0:T(8,128)(2,1)S(1)} %get-tuple-element.48), channel_id=1, source_target_pairs={{0,1},{1,2},{2,3},{3,4},{4,5},{5,6},{6,7},{7,8},{8,9},{9,10},{10,1... | collective-permute-start | bytes 1556 | tf_op jit(solution)/shard_map/ppermute | solution.py:25
  289.2 9.3 %collective-permute-start.11 = (bf16[258,1]{1,0:T(8,128)(2,1)S(1)}, bf16[258,1]{1,0:T(8,128)(2,1)S(1)}, u32[]{:S(2)}, u32[]{:S(2)}) collective-permute-start(bf16[258,1]{1,0:T(8,128)(2,1)S(1)} %get-tuple-element.49), channel_id=1, source_target_pairs={{1,0},{2,1},{3,2},{4,3},{5,4},{6,5},{7,6},{8,7},{9,8},{10,9},{11,1... | collective-permute-start | bytes 1556 | tf_op jit(solution)/shard_map/ppermute | solution.py:28
  352.3 25.6 %copy-start.10 = (f32[32,32]{1,0:T(8,128)S(1)}, f32[32,32]{1,0:T(8,128)}, u32[]{:S(2)}) copy-start(f32[32,32]{1,0:T(8,128)} %get-tuple-element.42) | copy-start | bytes 12292
  369.3 21.2 %collective-permute-start.4 = (bf16[1,32,1024]{2,1,0:T(8,128)(2,1)}, bf16[1,32,1024]{2,1,0:T(8,128)(2,1)}, u32[]{:S(2)}, u32[]{:S(2)}) collective-permute-start(bf16[1,32,1024]{2,1,0:T(8,128)(2,1)} %copy.150), channel_id=1, source_target_pairs={{0,16},{16,32},{32,48},{48,64},{64,80},{80,96},{96,112},{1,17},{17... | collective-permute-start | bytes 196616 | tf_op jit(solution)/shard_map/ppermute | solution.py:25
  373.7 16.8 %collective-permute-start.5 = (bf16[1,32,1024]{2,1,0:T(8,128)(2,1)}, bf16[1,32,1024]{2,1,0:T(8,128)(2,1)}, u32[]{:S(2)}, u32[]{:S(2)}) collective-permute-start(bf16[1,32,1024]{2,1,0:T(8,128)(2,1)} %copy.153), channel_id=1, source_target_pairs={{16,0},{32,16},{48,32},{64,48},{80,64},{96,80},{112,96},{17,1},{33... | collective-permute-start | bytes 196616 | tf_op jit(solution)/shard_map/ppermute | solution.py:28
  390.5 9.8 %copy-start.17 = (f32[32,32]{1,0:T(8,128)S(1)}, f32[32,32]{1,0:T(8,128)}, u32[]{:S(2)}) copy-start(f32[32,32]{1,0:T(8,128)} %get-tuple-element.45) | copy-start | bytes 12292
  391.5 10.8 %collective-permute-start.6 = (bf16[34,1,1024]{2,1,0:T(2,128)(2,1)S(1)}, bf16[34,1,1024]{2,1,0:T(2,128)(2,1)S(1)}, u32[]{:S(2)}, u32[]{:S(2)}) collective-permute-start(bf16[34,1,1024]{2,1,0:T(2,128)(2,1)S(1)} %get-tuple-element.12), channel_id=1, source_target_pairs={{0,1},{1,2},{2,3},{3,4},{4,5},{5,6},{6,7},{7,8},{8,9},{9,10},{10,1... | collective-permute-start | bytes 208904 | tf_op jit(solution)/shard_map/ppermute | solution.py:25
  396.6 10.0 %collective-permute-start.7 = (bf16[34,1,1024]{2,1,0:T(2,128)(2,1)S(1)}, bf16[34,1,1024]{2,1,0:T(2,128)(2,1)S(1)}, u32[]{:S(2)}, u32[]{:S(2)}) collective-permute-start(bf16[34,1,1024]{2,1,0:T(2,128)(2,1)S(1)} %get-tuple-element.13), channel_id=1, source_target_pairs={{1,0},{2,1},{3,2},{4,3},{5,4},{6,5},{7,6},{8,7},{9,8},{10,9},{11,1... | collective-permute-start | bytes 208904 | tf_op jit(solution)/shard_map/ppermute | solution.py:28
  400.4 8.8 %slice-start.2 = ((s8[4718592]{0:T(1024)(128)(4,1)}), s8[4194304]{0:T(1024)(128)(4,1)S(1)}, s32[]{:S(2)}) async-start(s8[4718592]{0:T(1024)(128)(4,1)} %bitcast.146), calls=%async_computation.5 | async-start | bytes 8388608
  402.4 6.8 %slice-start.3 = ((s8[4718592]{0:T(1024)(128)(4,1)}), s8[524288]{0:T(1024)(128)(4,1)S(1)}, s32[]{:S(2)}) async-start(s8[4718592]{0:T(1024)(128)(4,1)} %bitcast.146), calls=%async_computation.6 | async-start | bytes 1048576
  402.4 6.8 %copy-start.16 = (f32[32,32]{1,0:T(8,128)S(1)}, f32[32,32]{1,0:T(8,128)}, u32[]{:S(2)}) copy-start(f32[32,32]{1,0:T(8,128)} %get-tuple-element.40) | copy-start | bytes 12292
  409.2 0.8 copy-start.15
  409.2 1.5 copy-start.14
  410.7 0.8 copy-start.13
  411.5 0.8 copy-start.12
  412.3 0.8 copy-start.11
  427.5 12.8 %copy-start.5 = (f32[272,1,272]{2,0,1:T(8,128)S(1)}, f32[272,1,272]{2,0,1:T(8,128)}, u32[]{:S(2)}) copy-start(f32[272,1,272]{2,0,1:T(8,128)} %get-tuple-element.26) | copy-start | bytes 887812
  427.5 12.8 %copy-start.6 = (f32[272,1,272]{2,0,1:T(8,128)S(1)}, f32[272,1,272]{2,0,1:T(8,128)}, u32[]{:S(2)}) copy-start(f32[272,1,272]{2,0,1:T(8,128)} %get-tuple-element.27) | copy-start | bytes 887812
  427.5 12.8 %copy-start.7 = (f32[272,1,272]{2,0,1:T(8,128)S(1)}, f32[272,1,272]{2,0,1:T(8,128)}, u32[]{:S(2)}) copy-start(f32[272,1,272]{2,0,1:T(8,128)} %get-tuple-element.28) | copy-start | bytes 887812
  427.5 13.2 %copy-start.3 = (f32[257,257]{1,0:T(8,128)S(1)}, f32[257,257]{1,0:T(8,128)}, u32[]{:S(2)}) copy-start(f32[257,257]{1,0:T(8,128)} %get-tuple-element.36) | copy-start | bytes 792592
Sparse Core Ops, SparseCore 0:
  175.4 96.7 reduce-scatter.1
  275.3 55.3 all-gather.1
where the time goes:
time: 457 us; the launch traced here: 449 us
  local copies, waits for them, and re-layouts  154 us (34%)
  waiting for transfers between devices  145 us (32%)
  matrix products  68.9 us (15%)
  starting transfers between devices  44.7 us (10%)
  other arithmetic  20.5 us (4%)
  between operations  15 us (3%)
    reduce_scatter x1, waiting for transfers between devices, per_device(): lax.psum_scatter((flat_rows * norm_scale).reshape(height // lax.axis_size...  96.9 us
    dot_general x9, matrix products, per_device(): jnp.dot(source.reshape(block_rows * block_cols, FEAT), surrogate[offset],...  42.7 us
    all_gather x1, waiting for transfers between devices, per_device(): part_rows = lax.all_gather(far_miss, 'py', axis=0, tiled=True)  28.5 us
    reshape x1, local copies, waits for them, and re-layouts, field_rows(): shaped.transpose(0, 2, 3, 1, 4)  27.9 us
    ppermute x6, starting transfers between devices, with_halo(): lax.ppermute(lax.slice_in_dim(block, block.shape[dim] - width, None, axis...  26.4 us
    ppermute x6, waiting for transfers between devices, with_halo(): lax.ppermute(lax.slice_in_dim(block, 0, width, axis=dim), axis, backward)  19.2 us
    ppermute x6, starting transfers between devices, with_halo(): lax.ppermute(lax.slice_in_dim(block, 0, width, axis=dim), axis, backward)  18.2 us
    transpose x1, local copies, waits for them, and re-layouts, rows_field(): shaped.transpose(0, 3, 1, 2, 4)  16 us
  transfers between devices with their start and end apart: 14, of which 7 were waited for; matrix products, arithmetic and copies ran while one was open for 6% of the time, Pallas kernels for 0%

commit v1 on v0

--- a/solution.py
+++ b/solution.py
@@ -112,11 +112,43 @@
     return -(flow_down + flow_right)[1:, 1:] + flow_down[:-1, 1:] + flow_right[1:, :-1]
 
 
+def lane_perm():
+    rows = lax.broadcasted_iota(jnp.int32, (OUTS, OUTS), 0)
+    cols = lax.broadcasted_iota(jnp.int32, (OUTS, OUTS), 1)
+    inner = NW * BS
+    hit = (rows // (2 * BS) == cols % inner) & (rows % (2 * BS) == cols // inner)
+    return hit.astype(jnp.bfloat16)
+
+
+def dft_table(total_cols):
+    kk = jnp.arange(NK, dtype=jnp.int32) - NK // 2
+    low = 8 * BS
+    high = total_cols // low
+    a = jnp.arange(high, dtype=jnp.int32)
+    b = jnp.arange(low, dtype=jnp.int32)
+    scale = 2.0 * math.pi / total_cols
+    ta = ((a[:, None] * low * kk[None, :]) % total_cols).astype(jnp.float32) * scale
+    tb = ((b[:, None] * kk[None, :]) % total_cols).astype(jnp.float32) * scale
+    ca, sa = jnp.cos(ta), jnp.sin(ta)
+    cb, sb = jnp.cos(tb), jnp.sin(tb)
+    cb = cb.reshape(BS, BS, NK).transpose(1, 0, 2)
+    sb = sb.reshape(BS, BS, NK).transpose(1, 0, 2)
+    cos_v = ca[None, :, None, :] * cb[:, None, :, :] - sa[None, :, None, :] * sb[:, None, :, :]
+    sin_v = sa[None, :, None, :] * cb[:, None, :, :] + ca[None, :, None, :] * sb[:, None, :, :]
+    cos_v = cos_v.reshape(BS, total_cols // BS, NK)
+    sin_v = sin_v.reshape(BS, total_cols // BS, NK)
+    first = jnp.concatenate([cos_v, -sin_v], axis=-1)
+    second = jnp.concatenate([sin_v, cos_v], axis=-1)
+    table = jnp.stack([first, second]).astype(jnp.bfloat16)
+    return table.reshape(2 * BS, total_cols // BS, 2 * NK)
+
+
 def per_device(widths, couplings, surrogate, target_far):
     height, columns = widths.shape
     block_rows = height // BS
     block_cols = columns // BS
-    total_cols = columns * lax.axis_size("py")
+    groups = lax.axis_size("py")
+    total_cols = columns * groups
     total_rows = height * lax.axis_size("px")
     mask_cells = jnp.pad(couplings.astype(jnp.float32), ((0, 0), (0, 0), (0, BS * BS - 9)))
     mask_cells = (
@@ -127,51 +159,47 @@
     rimmed = with_halo(jnp.stack([widths, mask_cells]), (("px", 1), ("py", 2)), BS)
     wide_widths = rimmed[0]
     wide_mask = rimmed[1].reshape(block_rows + 2, BS, block_cols + 2, BS).transpose(0, 2, 1, 3)
-    wide_mask = wide_mask.reshape(block_rows + 2, block_cols + 2, BS * BS)
+    wide_mask = wide_mask.reshape(block_rows + 2, block_cols + 2, BS * BS).astype(jnp.bfloat16)
     values, slopes = chebyshev(wide_widths, NF)
     own_slopes = slopes[BS : BS + height, :, BS : BS + columns]
     features = cell_blocks(values, BS).astype(jnp.bfloat16)
-    gathered = jnp.zeros((block_rows, block_cols, OUTS), jnp.float32)
+    pieces = []
     for row_step in range(3):
         for col_step in range(3):
             offset = row_step * 3 + col_step
             source = features[
                 2 - row_step : 2 - row_step + block_rows, 2 - col_step : 2 - col_step + block_cols
             ]
-            product = jnp.dot(
-                source.reshape(block_rows * block_cols, FEAT),
-                surrogate[offset],
-                preferred_element_type=jnp.float32,
-            )
             flags = wide_mask[
                 2 - row_step : 2 - row_step + block_rows,
                 2 - col_step : 2 - col_step + block_cols,
                 offset,
             ]
-            gathered = gathered + flags[:, :, None] * product.reshape(block_rows, block_cols, OUTS)
-    near_field = gathered.astype(jnp.bfloat16)
-    row_flat = field_rows(near_field, BS, NW)
+            pieces.append(source * flags[:, :, None])
+    stacked = jnp.concatenate(pieces, axis=-1).reshape(block_rows * block_cols, 9 * FEAT)
+    near_field = jnp.dot(
+        stacked, surrogate.reshape(9 * FEAT, OUTS), preferred_element_type=jnp.float32
+    ).astype(jnp.bfloat16)
+    perm = lane_perm()
+    near_perm = jnp.dot(near_field, perm, preferred_element_type=jnp.float32).astype(jnp.bfloat16)
+    near_perm = near_perm.reshape(block_rows, block_cols, OUTS)
+    own_rows = lax.all_to_all(near_perm, "py", 0, 1, tiled=True)
+    own_bx = own_rows.shape[0]
+    all_by = own_rows.shape[1]
+    table = dft_table(total_cols)
     norm_scale = 1.0 / math.sqrt(total_cols)
-    local_table = phase_table(lax.axis_index("py") * columns, columns, total_cols)
-    part_rows = row_flat
-    flat_rows = jnp.dot(part_rows, local_table, preferred_element_type=jnp.float32)
-    far_field = lax.psum_scatter(
-        (flat_rows * norm_scale).reshape(
-            height // lax.axis_size("py") * lax.axis_size("py"), NW, 2, NK
-        ),
-        "py",
-        scatter_dimension=0,
-        tiled=True,
-    )
+    lhs = own_rows.reshape(own_bx, all_by, 2 * BS, NW * BS)
+    far_flat = jnp.einsum("bYpi,pYq->biq", lhs, table, preferred_element_type=jnp.float32)
+    far_field = (far_flat * norm_scale).reshape(own_bx * BS, NW, 2, NK)
     far_miss = (far_field - target_far.astype(jnp.float32)).astype(jnp.bfloat16)
-    part_rows = lax.all_gather(far_miss, "py", axis=0, tiled=True)
-    flat_rows = jnp.dot(
-        part_rows.reshape(part_rows.shape[0] * NW, 2 * NK),
-        local_table.T,
+    miss_flat = far_miss.reshape(own_bx, NW * BS, 2 * NK)
+    adj_flat = jnp.einsum("biq,pYq->bYpi", miss_flat, table, preferred_element_type=jnp.float32)
+    adj_perm = (adj_flat * norm_scale).astype(jnp.bfloat16).reshape(own_bx, all_by, OUTS)
+    adj_back = lax.all_to_all(adj_perm, "py", 1, 0, tiled=True)
+    adj_blocks = jnp.einsum(
+        "bc,rc->br", adj_back.reshape(block_rows * block_cols, OUTS), perm,
         preferred_element_type=jnp.float32,
-    )
-    adj_flat = (flat_rows * norm_scale).astype(jnp.bfloat16)
-    adj_blocks = rows_field(adj_flat, BS, NW)
+    ).astype(jnp.bfloat16).reshape(block_rows, block_cols, OUTS)
     wide_adj = with_halo(adj_blocks, (("px", 0), ("py", 1)), 1)
     feat_grad = jnp.zeros((block_rows, block_cols, FEAT), jnp.float32)
     for row_step in range(3):
@@ -191,7 +219,7 @@
             )
     planes = block_cells(feat_grad, BS, NF)
     near_grad = jnp.sum(planes * own_slopes, axis=1)
-    framed = with_halo(widths.astype(jnp.bfloat16), (("px", 0), ("py", 1)), 1).astype(widths.dtype)
+    framed = wide_widths[BS - 1 : BS + height + 1, BS - 1 : BS + columns + 1]
     grad_tv = variation(
         framed,
         lax.axis_index("px") * height,

time: 457 us -> 294 us (0.64)
  the two profiles are of different devices: /device:TPU:27 before, /device:TPU:121 now
where the time goes in v1:
time: 294 us; the launch traced here: 289 us
  local copies, waits for them, and re-layouts  99.8 us (34%)
  waiting for transfers between devices  60.7 us (21%)
  matrix products  46.5 us (16%)
  other arithmetic  45.1 us (15%)
  starting transfers between devices  35.2 us (12%)
    all_to_all x1, waiting for transfers between devices, per_device(): adj_back = lax.all_to_all(adj_perm, 'py', 1, 0, tiled=True)  25.8 us
    mul x9, local copies, waits for them, and re-layouts, per_device(): pieces.append(source * flags[:, :, None])  21 us
    ppermute x4, waiting for transfers between devices, with_halo(): lax.ppermute(lax.slice_in_dim(block, 0, width, axis=dim), axis, backward)  18.8 us
    ppermute x4, starting transfers between devices, with_halo(): lax.ppermute(lax.slice_in_dim(block, block.shape[dim] - width, None, axis...  15.1 us
    all_to_all x1, waiting for transfers between devices, per_device(): own_rows = lax.all_to_all(near_perm, 'py', 0, 1, tiled=True)  14.8 us
    unnamed x39, local copies, waits for them, and re-layouts  13.5 us
    reshape x1, local copies, waits for them, and re-layouts, block_cells(): shaped.transpose(0, 2, 3, 1, 4)  12.8 us
    dot_general x1, matrix products, per_device(): jnp.dot(near_field, perm, preferred_element_type=jnp.float32)  12.3 us
  transfers between devices with their start and end apart: 10, of which 6 were waited for; matrix products, arithmetic and copies ran while one was open for 9% of the time, Pallas kernels for 0%

profile of v1, /device:TPU:121, one launch (start us, length us, event | category | flops | bytes accessed | tf_op | source)
XLA Modules:
  0.0 288.7 jit_solution(7361475993336795754)
XLA Ops:
  1.7 2.7 copy.59
  4.4 4.0 %stack_reshape.3 = f32[1,256,256]{2,1,0:T(8,128)S(1)} reshape(f32[32,8,32,8]{3,2,1,0:T(8,128)} %bitcast.169) | data formatting | bytes 524288 | tf_op jit(solution)/shard_map/stack;reshape | solution.py:159
  8.5 1.9 collective-permute-start
  10.4 3.4 %collective-permute-start.1 = (f32[2,8,256]{2,1,0:T(8,128)S(1)}, f32[2,8,256]{2,1,0:T(8,128)S(1)}, u32[]{:S(2)}, u32[]{:S(2)}) collective-permute-start(f32[2,8,256]{2,1,0:T(8,128)S(1)} %get-tuple-element.54), channel_id=1, source_target_pairs={{16,0},{32,16},{48,32},{64,48},{80,64},{96,80},{112,96},{17,1},{33... | collective-permute-start | bytes 49160 | tf_op jit(solution)/shard_map/ppermute | solution.py:28
  15.3 5.7 %fusion.32 = (bf16[8,512,512]{2,1,0:T(8,128)(2,1)}, bf16[8,512,512]{2,1,0:T(8,128)(2,1)}, bf16[8,512,512]{2,1,0:T(8,128)(2,1)}) fusion(f32[8,8,512]{2,1,0:T(8,128)S(1)} %get-tuple-element.67, f32[512,512]{1,0:T(8,128)S(1)} %get-tuple-element.71, f32[8,8,512]{2,1,0:T(8,128)S(1)} %get-tuple-element.66, f32[512,512]{1,0:T(8,128)S(1)} %get-tuple-element.70), kind=kLoop, calls=%fused_computation.56 | loop fusion | flops 23068672 | bytes 14942208 | tf_op jit(solution)/shard_map/neg | solution.py:140
  21.2 5.4 %collective-permute-start.2 = (f32[2,272,8]{2,1,0:T(8,128)S(1)}, f32[2,272,8]{2,1,0:T(8,128)S(1)}, u32[]{:S(2)}, u32[]{:S(2)}) collective-permute-start(f32[2,272,8]{2,1,0:T(8,128)S(1)} %get-tuple-element.51), channel_id=1, source_target_pairs={{0,1},{1,2},{2,3},{3,4},{4,5},{5,6},{6,7},{7,8},{8,9},{9,10},{10,1... | collective-permute-start | bytes 52232 | tf_op jit(solution)/shard_map/ppermute | solution.py:25
  26.6 2.1 collective-permute-start.3
  30.1 8.0 %collective-permute-done.3 = f32[2,272,8]{2,1,0:T(8,128)S(1)} collective-permute-done((f32[2,272,8]{2,1,0:T(8,128)S(1)}, f32[2,272,8]{2,1,0:T(8,128)S(1)}, u32[]{:S(2)}, u32[]{:S(2)}) %collective-permute-start.3) | collective-permute-done | bytes 17440 | tf_op jit(solution)/shard_map/ppermute | solution.py:28
  39.4 3.2 %stack.31 = f32[34,8,1,34,8]{4,3,1,0,2:T(8,128)} reshape(f32[1,272,272]{2,1,0:T(8,128)S(1)} %get-tuple-element.38) | data formatting | bytes 591872 | tf_op jit(solution)/shard_map/stack | solution.py:45
  42.6 5.3 %copy.60 = f32[34,8,1,34,8]{3,4,2,1,0:T(8,128)} copy(f32[34,8,1,34,8]{4,3,1,0,2:T(8,128)} %stack.31) | data formatting | bytes 591872 | tf_op jit(solution)/shard_map/stack | solution.py:45
  47.9 3.2 %convert.15 = bf16[34,8,1,34,8]{4,3,1,0,2:T(8,128)(2,1)S(1)} convert(f32[34,8,1,34,8]{4,3,1,0,2:T(8,128)} %stack.31) | non-fusion elementwise | flops 73984 | bytes 443904 | tf_op jit(solution)/shard_map/convert.1
  53.9 3.5 %copy.63 = bf16[34,8,1,34,8]{3,4,2,1,0:T(8,128)(2,1)} copy(bf16[34,8,1,34,8]{4,3,1,0,2:T(8,128)(2,1)S(1)} %convert.15) | data formatting | bytes 295936 | tf_op jit(solution)/shard_map/convert.1
  59.2 3.5 %copy.64 = bf16[34,34,8,8]{1,3,2,0:T(8,128)(2,1)} copy(bf16[34,34,8,8]{3,1,2,0:T(8,128)(2,1)S(1)} %bitcast.170) | data formatting | bytes 295936 | tf_op jit(solution)/shard_map/convert_element_type | solution.py:162
  64.5 2.2 pad_maximum_fusion.1
  66.7 7.5 %slice_multiply_fusion = (bf16[32,32,256]{1,2,0:T(8,128)(2,1)S(1)}, bf16[32,32,256]{1,2,0:T(8,128)(2,1)}, bf16[32,32,256]{1,2,0:T(8,128)(2,1)}, bf16[32,32,256]{...) fusion(bf16[34,34,256]{1,2,0:T(8,128)(2,1)S(1)} %bitcast.165, ...), kind=kLoop, calls=%fused_computation.38 | loop fusion | flops 2359296 | bytes 9455616 | tf_op jit(solution)/shard_map/mul | solution.py:178
  76.9 2.6 copy.66
  79.5 2.6 copy.67
  82.1 2.6 copy.68
  84.6 2.6 copy.69
  87.2 2.6 copy.70
  89.8 2.6 copy.71
  94.2 1.9 copy.73
  96.2 2.0 constant_dynamic-update-slice_fusion.7
  98.2 1.9 constant_dynamic-update-slice_fusion.6
  100.1 1.9 constant_dynamic-update-slice_fusion.5
  102.0 1.9 constant_dynamic-update-slice_fusion.4
  107.4 12.3 %fusion.27 = bf16[1024,1024]{1,0:T(8,128)(2,1)} fusion(bf16[1024,2304]{1,0:T(8,128)(2,1)} %bitcast.190, bf16[2304,1024]{1,0:T(8,128)(2,1)} %bitcast.187, s32[1024]{0:T(1024)S(1)} %get-tuple-element.82, s32[1024]{0:T(1024)S(1)} %get-tuple-element.90, s32[1024]{0:T(1024)S(1)} %get-tuple-element.81, s32[1024]{0:T(1024)S(1)} %get-tuple-element.85, ...), kind=kOutput, calls=%fused_computation.49 | convolution fusion | flops 6988759040 | bytes 11571200 | tf_op jit(solution)/shard_map/dot_general | solution.py:184
  119.7 4.2 %all-to-all-start = ((bf16[32,32,1024]{2,1,0:T(8,128)(2,1)}), bf16[32,32,1024]{2,1,0:T(8,128)(2,1)S(1)}, u32[]{:S(2)}, u32[]{:S(2)}) async-start(bf16[32,32,1024]{2,1,0:T(8,128)(2,1)} %bitcast.184), calls=%async_computation | async-start | bytes 4194304 | tf_op jit(solution)/shard_map/all_to_all | solution.py:186
  123.9 7.7 %maximum_bitcast_fusion = (bf16[1,8,512,1024]{3,2,1,0:T(8,128)(2,1)S(1)}, bf16[1,8,512,1024]{3,2,1,0:T(8,128)(2,1)S(1)}) fusion(bf16[8,512,512]{2,1,0:T(8,128)(2,1)} %get-tuple-element.16, bf16[8,512,512]{2,1,0:T(8,128)(2,1)} %get-tuple-element.18, bf16[8,512,512]{2,1,0:T(8,128)(2,1)} %get-tuple-element.17), kind=kLoop, calls=%fused_computation.1 | loop fusion | flops 33554432 | bytes 29360128 | tf_op jit(solution)/shard_map/stack | solution.py:142
  131.6 6.7 %maximum_convert_fusion = bf16[2,8,512,1024]{3,2,1,0:T(8,128)(2,1)} fusion(bf16[1,8,512,1024]{3,2,1,0:T(8,128)(2,1)S(1)} %get-tuple-element.15, bf16[1,8,512,1024]{3,2,1,0:T(8,128)(2,1)S(1)} %get-tuple-element.14), kind=kLoop, calls=%fused_computation | loop fusion | flops 8388608 | bytes 33554432 | tf_op jit(solution)/shard_map/convert_element_type | solution.py:142
  138.3 14.8 %all-to-all-done = bf16[32,32,1024]{2,1,0:T(8,128)(2,1)S(1)} async-done(((bf16[32,32,1024]{2,1,0:T(8,128)(2,1)}), bf16[32,32,1024]{2,1,0:T(8,128)(2,1)S(1)}, u32[]{:S(2)}, u32[]{:S(2)}) %all-to-all-start) | async-done | bytes 2097184 | tf_op jit(solution)/shard_map/all_to_all | solution.py:186
  156.3 4.0 %reshape.369 = bf16[2,512,16,64]{3,2,1,0:T(8,128)(2,1)} reshape(bf16[2,16,32,1024]{3,2,1,0:T(8,128)(2,1)S(1)} %copy.74) | data formatting | bytes 4194304 | tf_op jit(solution)/shard_map/reshape | solution.py:191
  160.3 11.7 %fusion.84 = f32[2,64,1024]{2,1,0:T(8,128)S(1)} fusion(bf16[16,512,1024,1]{2,1,0,3:T(8,128)(2,1)} %bitcast.166, bf16[2,512,16,64]{3,2,1,0:T(8,128)(2,1)} %reshape.369), kind=kOutput, calls=%fused_computation.75 | convolution fusion | flops 2147614720 | bytes 19398656 | tf_op jit(solution)/shard_map/bYpi,pYq->biq/dot_general | solution.py:192
  173.6 11.4 %fusion.30 = bf16[2,512,16,64]{1,3,0,2:T(8,128)(2,1)S(1)} fusion(bf16[16,512,1024,1]{2,1,3,0:T(8,128)(2,1)} %bitcast.167, bf16[2,64,1024,1]{2,1,0,3:T(8,128)(2,1)S(1)} %reshape.379), kind=kOutput, calls=%fused_computation.51 | convolution fusion | flops 2149580800 | bytes 19136512 | tf_op jit(solution)/shard_map/biq,pYq->bYpi/dot_general | solution.py:196
  185.2 4.0 %copy.78 = bf16[2,512,1024]{2,0,1:T(2,128)(2,1)} copy(bf16[2,512,1024]{1,2,0:T(8,128)(2,1)S(1)} %bitcast.177) | data formatting | bytes 4194304 | tf_op jit(solution)/shard_map/reshape | solution.py:197
  189.2 6.3 %all-to-all-start.1 = ((bf16[2,512,1024]{2,0,1:T(2,128)(2,1)}), bf16[2,512,1024]{2,0,1:T(2,128)(2,1)S(1)}, u32[]{:S(2)}, u32[]{:S(2)}) async-start(bf16[2,512,1024]{2,0,1:T(2,128)(2,1)} %copy.78), calls=%async_computation.1 | async-start | bytes 4194304 | tf_op jit(solution)/shard_map/all_to_all | solution.py:198
  196.9 2.0 fusion.121
  198.9 25.8 %all-to-all-done.1 = bf16[2,512,1024]{2,0,1:T(2,128)(2,1)S(1)} async-done(((bf16[2,512,1024]{2,0,1:T(2,128)(2,1)}), bf16[2,512,1024]{2,0,1:T(2,128)(2,1)S(1)}, u32[]{:S(2)}, u32[]{:S(2)}) %all-to-all-start.1) | async-done | bytes 2097184 | tf_op jit(solution)/shard_map/all_to_all | solution.py:198
  225.5 4.0 %convolution_convert_fusion = bf16[1024,1024]{1,0:T(8,128)(2,1)S(1)} fusion(bf16[1024,1024]{1,0:T(8,128)(2,1)S(1)} %bitcast.185, s32[1024]{0:T(1024)S(1)} %get-tuple-element.82, s32[1024]{0:T(1024)S(1)} %get-tuple-element.90, s32[1024]{0:T(1024)S(1)} %get-tuple-element.81, s32[1024]{0:T(1024)S(1)} %get-tuple-element.85, s32[1024]{0:T(1024)S(1)} %get-tuple-element.83, ...), kind=kOutput, calls=%fused_computation.50 | convolution fusion | flops 2155872256 | bytes 4231168 | tf_op jit(solution)/shard_map/bc,rc->br/dot_general | solution.py:199
  229.6 4.5 %collective-permute-start.4 = (bf16[1,32,1024]{2,1,0:T(8,128)(2,1)S(1)}, bf16[1,32,1024]{2,1,0:T(8,128)(2,1)S(1)}, u32[]{:S(2)}, u32[]{:S(2)}) collective-permute-start(bf16[1,32,1024]{2,1,0:T(8,128)(2,1)S(1)} %get-tuple-element.32), channel_id=1, source_target_pairs={{0,16},{16,32},{32,48},{48,64},{64,80},{80,96},{96,112},{1,17},{17... | collective-permute-start | bytes 196616 | tf_op jit(solution)/shard_map/ppermute | solution.py:25
  234.1 1.9 collective-permute-start.5
  236.8 4.4 %collective-permute-done.5 = bf16[1,32,1024]{2,1,0:T(8,128)(2,1)S(1)} collective-permute-done((bf16[1,32,1024]{2,1,0:T(8,128)(2,1)S(1)}, bf16[1,32,1024]{2,1,0:T(8,128)(2,1)S(1)}, u32[]{:S(2)}, u32[]{:S(2)}) %collective-permute-start.5) | collective-permute-done | bytes 65568 | tf_op jit(solution)/shard_map/ppermute | solution.py:28
  241.4 3.3 %collective-permute-start.6 = (bf16[34,1,1024]{2,1,0:T(2,128)(2,1)S(1)}, bf16[34,1,1024]{2,1,0:T(2,128)(2,1)S(1)}, u32[]{:S(2)}, u32[]{:S(2)}) collective-permute-start(bf16[34,1,1024]{2,1,0:T(2,128)(2,1)S(1)} %get-tuple-element.21), channel_id=1, source_target_pairs={{0,1},{1,2},{2,3},{3,4},{4,5},{5,6},{6,7},{7,8},{8,9},{9,10},{10,1... | collective-permute-start | bytes 208904 | tf_op jit(solution)/shard_map/ppermute | solution.py:25
  244.7 2.1 collective-permute-start.7
  248.3 6.3 %collective-permute-done.7 = bf16[34,1,1024]{2,1,0:T(2,128)(2,1)S(1)} collective-permute-done((bf16[34,1,1024]{2,1,0:T(2,128)(2,1)S(1)}, bf16[34,1,1024]{2,1,0:T(2,128)(2,1)S(1)}, u32[]{:S(2)}, u32[]{:S(2)}) %collective-permute-start.7) | collective-permute-done | bytes 69664 | tf_op jit(solution)/shard_map/ppermute | solution.py:28
  261.2 2.7 copy.81
  263.9 10.6 %copy.82 = f32[32,8,4,32,8]{4,3,1,0,2:T(8,128)} copy(f32[32,8,4,32,8]{3,4,2,1,0:T(8,128)} %bitcast.168) | data formatting | bytes 2097152 | tf_op jit(solution)/shard_map/transpose | solution.py:61
  274.5 12.8 %reshape.376 = f32[256,4,256]{2,0,1:T(8,128)S(1)} reshape(f32[32,8,4,32,8]{4,3,1,0,2:T(8,128)} %copy.82) | data formatting | bytes 2097152 | tf_op jit(solution)/shard_map/reshape | solution.py:61
  (91 shorter events, 37.0 us)
Async XLA Ops:
  1.7 6.8 %copy-start.3 = (f32[256,256]{1,0:T(8,128)S(1)}, f32[256,256]{1,0:T(8,128)}, u32[]{:S(2)}) copy-start(f32[256,256]{1,0:T(8,128)} %param.4) | copy-start | bytes 786436
  8.5 12.5 %collective-permute-start = (f32[2,8,256]{2,1,0:T(8,128)S(1)}, f32[2,8,256]{2,1,0:T(8,128)S(1)}, u32[]{:S(2)}, u32[]{:S(2)}) collective-permute-start(f32[2,8,256]{2,1,0:T(8,128)S(1)} %get-tuple-element.53), channel_id=1, source_target_pairs={{0,16},{16,32},{32,48},{48,64},{64,80},{80,96},{96,112},{1,17},{17... | collective-permute-start | bytes 49160 | tf_op jit(solution)/shard_map/ppermute | solution.py:25
  10.4 10.6 %collective-permute-start.1 = (f32[2,8,256]{2,1,0:T(8,128)S(1)}, f32[2,8,256]{2,1,0:T(8,128)S(1)}, u32[]{:S(2)}, u32[]{:S(2)}) collective-permute-start(f32[2,8,256]{2,1,0:T(8,128)S(1)} %get-tuple-element.54), channel_id=1, source_target_pairs={{16,0},{32,16},{48,32},{64,48},{80,64},{96,80},{112,96},{17,1},{33... | collective-permute-start | bytes 49160 | tf_op jit(solution)/shard_map/ppermute | solution.py:28
  21.2 8.9 %collective-permute-start.2 = (f32[2,272,8]{2,1,0:T(8,128)S(1)}, f32[2,272,8]{2,1,0:T(8,128)S(1)}, u32[]{:S(2)}, u32[]{:S(2)}) collective-permute-start(f32[2,272,8]{2,1,0:T(8,128)S(1)} %get-tuple-element.51), channel_id=1, source_target_pairs={{0,1},{1,2},{2,3},{3,4},{4,5},{5,6},{6,7},{7,8},{8,9},{9,10},{10,1... | collective-permute-start | bytes 52232 | tf_op jit(solution)/shard_map/ppermute | solution.py:25
  26.6 11.5 %collective-permute-start.3 = (f32[2,272,8]{2,1,0:T(8,128)S(1)}, f32[2,272,8]{2,1,0:T(8,128)S(1)}, u32[]{:S(2)}, u32[]{:S(2)}) collective-permute-start(f32[2,272,8]{2,1,0:T(8,128)S(1)} %get-tuple-element.52), channel_id=1, source_target_pairs={{1,0},{2,1},{3,2},{4,3},{5,4},{6,5},{7,6},{8,7},{9,8},{10,9},{11,1... | collective-permute-start | bytes 52232 | tf_op jit(solution)/shard_map/ppermute | solution.py:28
  38.4 0.9 copy-start.2
  47.9 4.2 %copy-start.1 = (f32[34,8,1,34,8]{3,4,2,1,0:T(8,128)S(1)}, f32[34,8,1,34,8]{3,4,2,1,0:T(8,128)}, u32[]{:S(2)}) copy-start(f32[34,8,1,34,8]{3,4,2,1,0:T(8,128)} %copy.60) | copy-start | bytes 887812
  96.1 7.8 %copy-start.7 = (bf16[32,32,256]{2,1,0:T(8,128)(2,1)S(1)}, bf16[32,32,256]{2,1,0:T(8,128)(2,1)}, u32[]{:S(2)}) copy-start(bf16[32,32,256]{2,1,0:T(8,128)(2,1)} %copy.70) | copy-start | bytes 1572868
  96.1 8.6 %copy-start.6 = (bf16[32,32,256]{2,1,0:T(8,128)(2,1)S(1)}, bf16[32,32,256]{2,1,0:T(8,128)(2,1)}, u32[]{:S(2)}) copy-start(bf16[32,32,256]{2,1,0:T(8,128)(2,1)} %copy.71) | copy-start | bytes 1572868
  96.1 10.4 %copy-start.5 = (bf16[32,32,256]{2,1,0:T(8,128)(2,1)S(1)}, bf16[32,32,256]{2,1,0:T(8,128)(2,1)}, u32[]{:S(2)}) copy-start(bf16[32,32,256]{2,1,0:T(8,128)(2,1)} %copy.73) | copy-start | bytes 1572868
  119.7 33.5 %all-to-all-start = ((bf16[32,32,1024]{2,1,0:T(8,128)(2,1)}), bf16[32,32,1024]{2,1,0:T(8,128)(2,1)S(1)}, u32[]{:S(2)}, u32[]{:S(2)}) async-start(bf16[32,32,1024]{2,1,0:T(8,128)(2,1)} %bitcast.184), calls=%async_computation | async-start | bytes 4194304 | tf_op jit(solution)/shard_map/all_to_all | solution.py:186
  153.2 1.3 copy-start
  160.3 11.7 %copy-start.10 = (bf16[16,8,2,512]{3,2,1,0:T(2,128)(2,1)S(1)}, bf16[16,8,2,512]{3,2,1,0:T(2,128)(2,1)}, u32[]{:S(2)}) copy-start(bf16[16,8,2,512]{3,2,1,0:T(2,128)(2,1)} %param.7) | copy-start | bytes 786436
  185.2 10.4 %copy-start.9 = (s32[32,32,9]{1,0,2:T(8,128)S(1)}, s32[32,32,9]{1,0,2:T(8,128)}, u32[]{:S(2)}) copy-start(s32[32,32,9]{1,0,2:T(8,128)} %param.5) | copy-start | bytes 110596
  189.2 35.5 %all-to-all-start.1 = ((bf16[2,512,1024]{2,0,1:T(2,128)(2,1)}), bf16[2,512,1024]{2,0,1:T(2,128)(2,1)S(1)}, u32[]{:S(2)}, u32[]{:S(2)}) async-start(bf16[2,512,1024]{2,0,1:T(2,128)(2,1)} %copy.78), calls=%async_computation.1 | async-start | bytes 4194304 | tf_op jit(solution)/shard_map/all_to_all | solution.py:198
  225.3 10.7 %slice-start = ((s8[4718592]{0:T(1024)(128)(4,1)}), s8[4194304]{0:T(1024)(128)(4,1)S(1)}, s32[]{:S(2)}) async-start(s8[4718592]{0:T(1024)(128)(4,1)} %bitcast.188), calls=%async_computation.2 | async-start | bytes 8388608
  225.5 10.5 %slice-start.1 = ((s8[4718592]{0:T(1024)(128)(4,1)}), s8[524288]{0:T(1024)(128)(4,1)S(1)}, s32[]{:S(2)}) async-start(s8[4718592]{0:T(1024)(128)(4,1)} %bitcast.188), calls=%async_computation.3 | async-start | bytes 1048576
  229.6 7.2 %collective-permute-start.4 = (bf16[1,32,1024]{2,1,0:T(8,128)(2,1)S(1)}, bf16[1,32,1024]{2,1,0:T(8,128)(2,1)S(1)}, u32[]{:S(2)}, u32[]{:S(2)}) collective-permute-start(bf16[1,32,1024]{2,1,0:T(8,128)(2,1)S(1)} %get-tuple-element.32), channel_id=1, source_target_pairs={{0,16},{16,32},{32,48},{48,64},{64,80},{80,96},{96,112},{1,17},{17... | collective-permute-start | bytes 196616 | tf_op jit(solution)/shard_map/ppermute | solution.py:25
  234.1 7.1 %collective-permute-start.5 = (bf16[1,32,1024]{2,1,0:T(8,128)(2,1)S(1)}, bf16[1,32,1024]{2,1,0:T(8,128)(2,1)S(1)}, u32[]{:S(2)}, u32[]{:S(2)}) collective-permute-start(bf16[1,32,1024]{2,1,0:T(8,128)(2,1)S(1)} %get-tuple-element.33), channel_id=1, source_target_pairs={{16,0},{32,16},{48,32},{64,48},{80,64},{96,80},{112,96},{17,1},{33... | collective-permute-start | bytes 196616 | tf_op jit(solution)/shard_map/ppermute | solution.py:28
  241.4 6.9 %collective-permute-start.6 = (bf16[34,1,1024]{2,1,0:T(2,128)(2,1)S(1)}, bf16[34,1,1024]{2,1,0:T(2,128)(2,1)S(1)}, u32[]{:S(2)}, u32[]{:S(2)}) collective-permute-start(bf16[34,1,1024]{2,1,0:T(2,128)(2,1)S(1)} %get-tuple-element.21), channel_id=1, source_target_pairs={{0,1},{1,2},{2,3},{3,4},{4,5},{5,6},{6,7},{7,8},{8,9},{9,10},{10,1... | collective-permute-start | bytes 208904 | tf_op jit(solution)/shard_map/ppermute | solution.py:25
  244.7 10.0 %collective-permute-start.7 = (bf16[34,1,1024]{2,1,0:T(2,128)(2,1)S(1)}, bf16[34,1,1024]{2,1,0:T(2,128)(2,1)S(1)}, u32[]{:S(2)}, u32[]{:S(2)}) collective-permute-start(bf16[34,1,1024]{2,1,0:T(2,128)(2,1)S(1)} %get-tuple-element.22), channel_id=1, source_target_pairs={{1,0},{2,1},{3,2},{4,3},{5,4},{6,5},{7,6},{8,7},{9,8},{10,9},{11,1... | collective-permute-start | bytes 208904 | tf_op jit(solution)/shard_map/ppermute | solution.py:28
  274.5 12.8 %copy-start.8 = (f32[272,1,272]{2,0,1:T(8,128)S(1)}, f32[272,1,272]{2,0,1:T(8,128)}, u32[]{:S(2)}) copy-start(f32[272,1,272]{2,0,1:T(8,128)} %get-tuple-element.41) | copy-start | bytes 887812
  274.5 13.1 %copy-start.4 = (f32[257,257]{1,0:T(8,128)S(1)}, f32[257,257]{1,0:T(8,128)}, u32[]{:S(2)}) copy-start(f32[257,257]{1,0:T(8,128)} %get-tuple-element.56) | copy-start | bytes 792592
